TPU v7x, 256 devices: a whole 4x4x8 slice. The times are simulated.
256 devices in a mesh: seq: 64 (over z, y, x_lo), head: 4 (over x_hi, core).
Axes of the slice: x: 4 (x_hi: 2, x_lo: 2; x = x_hi * 2 + x_lo), y: 4, z: 8, core: 2. Of those that a mesh axis runs over, the one named last changes fastest.
Arguments:
- features: bfloat16 [8192, 960], P('seq', 'head'), may hold values from -36 to 36
- conv_weight: bfloat16 [960, 120, 128], P('head'), may hold values from -0.046875 to 0.046875
- ln_gain: float32 [960], replicated, may hold values from 0.5 to 1.5
- ln_bias: float32 [960], replicated, may hold values from -4 to 4
- query_weight: bfloat16 [8, 115200], P('head'), may hold values from -0.875 to 0.875
- key_weight: bfloat16 [8, 115200], P('head'), may hold values from -0.875 to 0.875
- value_weight: bfloat16 [8, 115200], P('head'), may hold values from -0.1875 to 0.1875
- out_weight: bfloat16 [960, 960], P('head'), may hold values from -0.1875 to 0.1875
- proj_weight: bfloat16 [960, 1024], P(None, 'head'), may hold values from -0.10085894 to 0.10085894
- targets: bfloat16 [8192, 1024], P('seq', 'head'), may hold values from -3.125 to 3.125
- mask_positions: int32 [1024], P('seq'), may hold values from 0 to 8191, as said below
- distractors: int32 [1024, 100], P('seq'), may hold values from 0 to 8191, as said below
- loss_weight: float32 [1024], P('seq'), may hold values from 0.2 to 2
Outputs:
- encoded: bfloat16 [8192, 960], P('seq', 'head')
- proj_grad: float32 [960, 1024], P(None, 'head')
- target_grad: float32 [8192, 1024], P('seq', 'head')
Inputs may be any that keep to these rules, and one draw needn't show every extreme that they name: `mask_positions`: the entries of aligned block d of 16 are distinct frames of d * 128 to (d + 1) * 128 - 1. `distractors`: call value // 128 the block of an entry. In every aligned block of 16 rows exactly 50 entries name one block, the same block for all row blocks and drawn from the seed; the remaining 16 * 100 - 50 entries of the row block are spread over the other blocks as evenly as possible.
All inputs are finite; a program needn't handle non-finite values.
Results may differ from a plain program's by a relative error of at most 0.007.
Values may be sent and summed in bfloat16 or wider, within the bound.
No kernel may reach another device: no remote copies, remote signals or barrier semaphores. Data moves between devices by JAX's collectives and lax.ppermute only.
A program may use at most 128 MiB of HBM per device.

v0:
```python
import math

import jax
import jax.numpy as jnp
from jax import lax
from jax.sharding import PartitionSpec as P

TAPS = 128


NORM_EPS = 1e-05
EPSILON = 1e-06
SOFTMAX_WARMTH = 0.1


def with_halo(shard, sides, width):
    for axis, dim in sides:
        size, length = (lax.axis_size(axis), shard.shape[dim])
        up = [(i, (i + 1) % size) for i in range(size - 1)]
        down = [(j, i) for i, j in up]
        last = lax.slice_in_dim(shard, length - width, length, axis=dim)
        first = lax.slice_in_dim(shard, 0, width, axis=dim)
        before = lax.ppermute(last, axis, up)
        after = lax.ppermute(first, axis, down)
        shard = jnp.concatenate([before, shard, after], axis=dim)
    return shard


def layer_norm(hidden, gain_terms, bias_terms):
    wide = hidden.astype(jnp.float32)
    center = jnp.mean(wide, axis=-1, keepdims=True)
    spread = jnp.mean((wide - center) ** 2, axis=-1, keepdims=True)
    return ((wide - center) * lax.rsqrt(spread + NORM_EPS) * gain_terms + bias_terms).astype(
        jnp.bfloat16
    )


def head_project(normed, flat_weight, head_count, head_dim):
    full_width = normed.shape[1]
    head_weight = flat_weight.reshape(head_count, full_width, head_dim)
    result = jnp.einsum("tw,hwd->thd", normed, head_weight, preferred_element_type=jnp.float32)
    return result.astype(jnp.bfloat16)


def contrast_terms(products, target_sq, context_sq, weight_matrix):
    inv_context = lax.rsqrt(context_sq + EPSILON)
    inv_target = lax.rsqrt(target_sq + EPSILON)
    cosine_scores = products * inv_context[:, None] * inv_target
    exponentiated = jnp.exp(cosine_scores / SOFTMAX_WARMTH)
    softmax_shares = exponentiated / jnp.sum(exponentiated, axis=1, keepdims=True)
    leading_term = (lax.broadcasted_iota(jnp.int32, softmax_shares.shape, 1) == 0).astype(
        jnp.float32
    )
    logit_slope = weight_matrix[:, None] * (softmax_shares - leading_term) / SOFTMAX_WARMTH
    along = logit_slope * inv_context[:, None] * inv_target
    shrink = logit_slope * cosine_scores * inv_target * inv_target
    spread = jnp.sum(logit_slope * cosine_scores, axis=1) * inv_context * inv_context
    return (along, shrink, spread)


def attend_block(running, key_block, value_block, query_heads, head_count, score_scale):
    numer, denom, highest = running
    row_count = key_block.shape[0]
    key_heads = key_block.reshape(row_count, head_count, -1)
    value_heads = value_block.reshape(row_count, head_count, -1)
    scores = (
        jnp.einsum("qhd,khd->hqk", query_heads, key_heads, preferred_element_type=jnp.float32)
        * score_scale
    )
    new_high = jnp.maximum(highest, jnp.max(scores, axis=2))
    factor = jnp.exp(highest - new_high)
    weights = jnp.exp(scores - new_high[:, :, None])
    denom = denom * factor + jnp.sum(weights, axis=2)
    numer = numer * factor[:, :, None] + jnp.einsum(
        "hqk,khd->hqd",
        weights.astype(jnp.bfloat16),
        value_heads,
        preferred_element_type=jnp.float32,
    )
    return (numer, denom, new_high)


def take_rows(asked, targets):
    return targets[jnp.maximum(asked, 0)]


def place_rows(asked_flat, rows_flat, frame_count):
    segment_ids = jnp.where(asked_flat >= 0, asked_flat, frame_count)
    return jax.ops.segment_sum(rows_flat, segment_ids, num_segments=frame_count + 1)[:frame_count]


def per_device(
    features,
    conv_weight,
    ln_gain,
    ln_bias,
    query_weight,
    key_weight,
    value_weight,
    out_weight,
    proj_weight,
    targets,
    mask_positions,
    distractors,
    loss_weight,
):
    frame_count, local_width = features.shape
    head_dim = conv_weight.shape[1]
    head_count = local_width // head_dim
    extended = with_halo(features, (("seq", 0),), TAPS // 2)
    position = lax.conv_general_dilated(
        extended[None],
        conv_weight,
        (1,),
        "VALID",
        dimension_numbers=("NWC", "OIW", "NWC"),
        feature_group_count=head_count,
        preferred_element_type=jnp.float32,
    )[0, :frame_count]
    hidden = (features.astype(jnp.float32) + jax.nn.gelu(position, approximate=False)).astype(
        jnp.bfloat16
    )
    normed = layer_norm(lax.all_gather(hidden, "head", axis=1, tiled=True), ln_gain, ln_bias)
    query_heads = head_project(normed, query_weight, head_count, head_dim)
    key_here = head_project(normed, key_weight, head_count, head_dim).reshape(
        frame_count, local_width
    )
    value_here = head_project(normed, value_weight, head_count, head_dim).reshape(
        frame_count, local_width
    )
    score_scale = 1.0 / math.sqrt(head_dim)
    initial = (
        jnp.zeros((head_count, frame_count, head_dim), jnp.float32),
        jnp.zeros((head_count, frame_count), jnp.float32),
        jnp.full((head_count, frame_count), -1e30, jnp.float32),
    )
    running = initial
    key_piece = lax.all_gather(key_here, "seq", axis=0, tiled=True)
    value_piece = lax.all_gather(value_here, "seq", axis=0, tiled=True)
    row_count = key_piece.shape[0]

    def advance(partial_value, blocks):
        return (
            attend_block(partial_value, blocks[0], blocks[1], query_heads, head_count, score_scale),
            None,
        )

    running, _ = lax.scan(
        advance,
        running,
        (
            key_piece.reshape(row_count // 512, 512, -1),
            value_piece.reshape(row_count // 512, 512, -1),
        ),
    )
    numer, denom, _ = running
    attended = (
        (numer / denom[:, :, None])
        .astype(jnp.bfloat16)
        .transpose(1, 0, 2)
        .reshape(frame_count, local_width)
    )
    branch = lax.psum_scatter(
        jnp.dot(attended, out_weight, preferred_element_type=jnp.float32).astype(jnp.bfloat16),
        "head",
        scatter_dimension=1,
        tiled=True,
    ).astype(jnp.float32)
    encoded = (hidden.astype(jnp.float32) + branch).astype(jnp.bfloat16)
    seq_index = lax.axis_index("seq")
    seq_count = lax.axis_size("seq")
    local_mask = mask_positions - seq_index * frame_count
    masked_full = lax.all_gather(encoded[local_mask], "head", axis=1, tiled=True)
    context = jnp.dot(masked_full, proj_weight, preferred_element_type=jnp.float32)
    masked_count, distract_count = distractors.shape
    request_count = masked_count * distract_count
    capacity = 2 * request_count // seq_count
    target_width = targets.shape[1]
    flat_dist = distractors.reshape(-1)
    owners = flat_dist // frame_count
    row_ids = flat_dist % frame_count
    owner_hits = (owners[:, None] == jnp.arange(seq_count, dtype=jnp.int32)[None, :]).astype(
        jnp.int32
    )
    earlier = jnp.cumsum(owner_hits, axis=0) - owner_hits
    slot_ids = jnp.sum(earlier * owner_hits, axis=1)
    buckets = owners * capacity + slot_ids
    requests = (
        jnp.full((seq_count * capacity,), -1, jnp.int32)
        .at[buckets]
        .set(row_ids)
        .reshape(seq_count, capacity)
    )
    positive = targets[local_mask]
    asked = lax.all_to_all(requests, "seq", split_axis=0, concat_axis=0, tiled=True)
    found = take_rows(asked, targets)
    returned = lax.all_to_all(found, "seq", split_axis=0, concat_axis=0, tiled=True)
    fetched = returned.reshape(seq_count * capacity, target_width)[buckets].reshape(
        masked_count, distract_count, target_width
    )
    cands = jnp.concatenate([positive[:, None, :], fetched], axis=1).astype(jnp.float32)
    products_here = jnp.einsum("me,mke->mk", context, cands, precision=lax.Precision.HIGHEST)
    target_sq_here = jnp.sum(cands * cands, axis=2)
    context_sq_here = jnp.sum(context * context, axis=1)
    products, target_sq, context_sq = lax.psum(
        (products_here, target_sq_here, context_sq_here), "head"
    )
    along, shrink, spread = contrast_terms(products, target_sq, context_sq, loss_weight)
    cand_grads = along[:, :, None] * context[:, None, :] - shrink[:, :, None] * cands
    context_grad = (
        jnp.einsum("mk,mke->me", along, cands, precision=lax.Precision.HIGHEST)
        - spread[:, None] * context
    )
    target_grad = (
        jnp.zeros((frame_count, target_width), jnp.float32).at[local_mask].add(cand_grads[:, 0])
    )
    outgoing = (
        jnp.zeros((seq_count * capacity, target_width), jnp.float32)
        .at[buckets]
        .set(cand_grads[:, 1:].reshape(request_count, target_width))
    )
    incoming = (
        lax.all_to_all(
            outgoing.reshape(seq_count, capacity, target_width).astype(jnp.bfloat16),
            "seq",
            split_axis=0,
            concat_axis=0,
            tiled=True,
        )
        .astype(jnp.float32)
        .reshape(seq_count * capacity, target_width)
    )
    target_grad = target_grad + place_rows(asked.reshape(-1), incoming, frame_count)
    proj_term = jnp.einsum(
        "mw,me->we", masked_full.astype(jnp.float32), context_grad, precision=lax.Precision.HIGHEST
    )
    proj_grad = lax.psum(proj_term, "seq")
    return (encoded, proj_grad, target_grad)


def solution(mesh):
    return jax.shard_map(
        per_device,
        mesh=mesh,
        in_specs=(
            P("seq", "head"),
            P("head", None, None),
            P(),
            P(),
            P("head", None),
            P("head", None),
            P("head", None),
            P("head", None),
            P(None, "head"),
            P("seq", "head"),
            P("seq"),
            P("seq", None),
            P("seq"),
        ),
        out_specs=(P("seq", "head"), P(None, "head"), P("seq", "head")),
        check_vma=False,
    )
```

profile of v0, /device:TPU:8, one launch (start us, length us, event | category | flops | bytes accessed | tf_op | source)
XLA Modules:
  0.0 1307.5 jit_solution(7271690625776360250)
XLA Ops:
  8.2 3.4 collective-permute-start
  15.0 10.7 copy.41
  27.6 17.3 %fusion.67 = f32[1,129,2,120]{3,0,2,1:T(1,128)S(1)} fusion(bf16[1,256,2,120]{3,0,2,1:T(2,128)(2,1)S(1)} %copy.40, bf16[2,120,120,128]{2,1,0,3:T(8,128)(2,1)} %copy.41), kind=kOutput, calls=%fused_computation.135 | convolution fusion | flops 951091200 | bytes 7619520 | tf_op jit(solution)/shard_map/conv_general_dilated | solution.py:111
  45.3 7.2 all_gather.12
  57.4 18.1 %reduce-window.6 = s32[64,13,128]{2,1,0:T(8,128)S(1)} reduce-window(s32[64,13,128]{2,1,0:T(8,128)S(1)} %reshape.259, s32[]{:T(128)} %constant.57.clone.1), window={size=1x1x128 pad=0_0x0_0x127_0}, to_apply=%region_7.8 | reduce-window | flops 13524992 | bytes 851972 | tf_op jit(solution)/shard_map/reduce-window
  76.7 8.8 scatter_custom_fusion
  86.3 12.8 all-to-all-start
  100.6 7.8 all-to-all-done
  110.0 9.9 gather_fusion.2
  121.4 6.3 all-to-all-start.1
  128.5 194.0 %all-gather.7.cloned.1.call-done = bf16[8192,240]{0,1:T(8,128)(2,1)} async-done(((bf16[128,240]{0,1:T(8,128)(2,1)}), bf16[8192,240]{0,1:T(8,128)(2,1)}) %all-gather.7.cloned.1.call-update) | async-done | bytes 3932176 | tf_op jit(solution)/shard_map/all_gather | solution.py:139
  322.5 4.4 copy.77
  326.9 243.4 %all-gather.5.cloned.1.call-done = bf16[8192,240]{0,1:T(8,128)(2,1)} async-done(((bf16[128,240]{0,1:T(8,128)(2,1)}), bf16[8192,240]{0,1:T(8,128)(2,1)}) %all-gather.5.cloned.1.call-update) | async-done | bytes 3932176 | tf_op jit(solution)/shard_map/all_gather | solution.py:138
  570.3 4.4 copy.78
  574.8 29.4 %while.15 = (s32[]{:T(128)}, f32[2,128,120]{1,2,0:T(8,128)S(1)}, f32[2,128]{1,0:T(2,128)S(1)}, f32[2,128]{1,0:T(2,128)S(1)}, bf16[16,512,240]{1,2,0:T(8,128)(2,1...) while((s32[]{:T(128)}, f32[2,128,120]{1,2,0:T(8,128)S(1)}, ...), condition=%wide.region_5.6_spmd.clone, body=%wide.region_2.5_spmd.clone.sunk | while | flops 63794432 | bytes 3371117 | solution.py:148
  608.5 5.6 gather_fusion.3
  614.7 20.9 %reduce-scatter.2.cloned.1.call-done = bf16[128,240]{0,1:T(8,128)(2,1)} async-done(((bf16[128,960]{0,1:T(8,128)(2,1)}), bf16[128,240]{0,1:T(8,128)(2,1)}) %reduce-scatter.2.cloned.1.call-update) | async-done | bytes 61456 | tf_op jit(solution)/shard_map/reduce_scatter | solution.py:163
  637.1 6.7 all-gather.1
  645.1 13.6 %all-reduce.1 = (f32[16,101]{1,0:T(8,128)S(1)}, f32[16]{0:T(128)S(1)}, f32[16,101]{1,0:T(8,128)S(1)}) all-reduce(f32[16,101]{1,0:T(8,128)S(1)} %fusion.7, f32[16]{0:T(128)S(1)} %get-tuple-element.115, f32[16,101]{1,0:T(8,128)S(1)} %bitcast.173), channel_id=1, replica_groups=mesh['seq'=64,'head'=4] {'head'}, use_global_device_ids=true, to_apply=%region_15.16 | all-reduce | flops 3248 | bytes 25984 | tf_op jit(solution)/shard_map/psum | solution.py:205
  662.4 12.8 scatter_custom_fusion.1
  678.8 11.5 all-to-all-start.2
  693.8 40.9 %all-to-all-done.2 = bf16[64,50,256]{2,1,0:T(8,128)(2,1)S(1)} async-done(((bf16[64,50,256]{2,1,0:T(8,128)(2,1)}), bf16[64,50,256]{2,1,0:T(8,128)(2,1)S(1)}, u32[]{:S(2)}, u32[]{:S(2)}) %all-to-all-start.2) | async-done | bytes 1638432 | tf_op jit(solution)/shard_map/all_to_all | solution.py:223
  736.7 20.7 %scatter_custom_fusion.2 = f32[129,256]{1,0:T(8,128)S(1)} fusion(s32[3200]{0:T(1024)S(1)} %fusion.48, f32[3200,256]{1,0:T(8,128)} %reshape.314, f32[]{:T(128)} %constant.68.clone.1), kind=kCustom, calls=%fused_computation.78 | custom fusion | flops 819200 | bytes 132608 | tf_op jit(solution)/shard_map/scatter-add | solution.py:89
  758.2 540.6 %all-reduce.4.cloned.1.call-done = f32[960,256]{1,0:T(8,128)} async-done(((f32[960,256]{1,0:T(8,128)}), f32[960,256]{1,0:T(8,128)}) %all-reduce.4.cloned.1.call-update) | async-done | bytes 983056 | tf_op jit(solution)/shard_map/psum | solution.py:237
  (234 shorter events, 70.5 us)
Async XLA Ops:
  7.2 597.1 %copy-start = (bf16[240,960]{1,0:T(8,128)(2,1)S(1)}, bf16[240,960]{1,0:T(8,128)(2,1)}, u32[]{:S(2)}) copy-start(bf16[240,960]{1,0:T(8,128)(2,1)} %param.22) | copy-start | bytes 1382404
  7.2 315.4 %all-gather.7.cloned.1.call-start = ((), (), s32[]{:S(2)}) async-start(), calls=%async_computation.5 | async-start | bytes 3993600 | tf_op jit(solution)/shard_map/all_gather | solution.py:139
  8.2 19.0 %collective-permute-start = (bf16[64,240]{0,1:T(8,128)(2,1)S(1)}, bf16[64,240]{0,1:T(8,128)(2,1)S(1)}, u32[]{:S(2)}, u32[]{:S(2)}) collective-permute-start(bf16[64,240]{0,1:T(8,128)(2,1)S(1)} %get-tuple-element.106), channel_id=1, source_target_pairs={{0,4},{4,8},{8,12},{12,16},{16,20},{20,24},{24,28},{28,32},{32,36}... | collective-permute-start | bytes 92168 | tf_op jit(solution)/shard_map/ppermute | solution.py:23
  11.6 15.6 %collective-permute-start.1 = (bf16[64,240]{0,1:T(8,128)(2,1)S(1)}, bf16[64,240]{0,1:T(8,128)(2,1)S(1)}, u32[]{:S(2)}, u32[]{:S(2)}) collective-permute-start(bf16[64,240]{0,1:T(8,128)(2,1)S(1)} %get-tuple-element.107), channel_id=1, source_target_pairs={{4,0},{8,4},{12,8},{16,12},{20,16},{24,20},{28,24},{32,28},{36,32}... | collective-permute-start | bytes 92168 | tf_op jit(solution)/shard_map/ppermute | solution.py:24
  15.0 10.8 copy-start.5
  25.7 1.5 copy-start.3
  27.6 25.3 %copy-start.12 = (f32[960]{0:T(1024)S(1)}, f32[960]{0:T(1024)}, u32[]{:S(2)}) copy-start(f32[960]{0:T(1024)} %param.18) | copy-start | bytes 11524
  27.6 25.3 %copy-start.13 = (f32[960]{0:T(1024)S(1)}, f32[960]{0:T(1024)}, u32[]{:S(2)}) copy-start(f32[960]{0:T(1024)} %param.17) | copy-start | bytes 11524
  44.9 9.4 copy-start.6
  54.1 3.0 copy-start.10
  54.1 516.2 %all-gather.5.cloned.1.call-start = ((), (), s32[]{:S(2)}) async-start(), calls=%async_computation.4 | async-start | bytes 3993600 | tf_op jit(solution)/shard_map/all_gather | solution.py:138
  75.8 23.3 %copy-start.7 = (bf16[2,115200]{1,0:T(2,128)(2,1)S(1)}, bf16[2,115200]{1,0:T(2,128)(2,1)}, u32[]{:S(2)}) copy-start(bf16[2,115200]{1,0:T(2,128)(2,1)} %param.19) | copy-start | bytes 1382404
  76.4 33.5 %copy-start.1 = (bf16[128,256]{1,0:T(8,128)(2,1)S(1)}, bf16[128,256]{1,0:T(8,128)(2,1)}, u32[]{:S(2)}) copy-start(bf16[128,256]{1,0:T(8,128)(2,1)} %param.24) | copy-start | bytes 196612
  86.3 22.2 %all-to-all-start = ((s32[64,1,50]{2,1,0:T(1,128)}), s32[64,1,50]{2,1,0:T(1,128)S(1)}, u32[]{:S(2)}, u32[]{:S(2)}) async-start(s32[64,1,50]{2,1,0:T(1,128)} %bitcast.24), calls=%async_computation.1 | async-start | bytes 65536 | tf_op jit(solution)/shard_map/all_to_all | solution.py:195
  121.4 484.6 %all-to-all-start.1 = ((bf16[64,50,256]{2,1,0:T(8,128)(2,1)}), bf16[64,50,256]{2,1,0:T(8,128)(2,1)}, u32[]{:S(2)}, u32[]{:S(2)}) async-start(bf16[64,50,256]{2,1,0:T(8,128)(2,1)} %reshape.279), calls=%async_computation.2 | async-start | bytes 3670016 | tf_op jit(solution)/shard_map/all_to_all | solution.py:197
  127.7 507.9 %reduce-scatter.2.cloned.1.call-start = ((), (), s32[]{:S(2)}) async-start(), calls=%async_computation.6 | async-start | bytes 307200 | tf_op jit(solution)/shard_map/reduce_scatter | solution.py:163
  574.8 30.6 %copy-start.14 = (s32[16]{0:T(128)S(1)}, s32[16]{0:T(128)}, u32[]{:S(2)}) copy-start(s32[16]{0:T(128)} %param.25) | copy-start | bytes 196
  614.1 29.9 %copy-start.4 = (bf16[960,256]{1,0:T(8,128)(2,1)S(1)}, bf16[960,256]{1,0:T(8,128)(2,1)}, u32[]{:S(2)}) copy-start(bf16[960,256]{1,0:T(8,128)(2,1)} %param.23) | copy-start | bytes 1474564
  614.3 44.5 %copy-start.11 = (f32[16]{0:T(128)S(1)}, f32[16]{0:T(128)}, u32[]{:S(2)}) copy-start(f32[16]{0:T(128)} %param.27) | copy-start | bytes 196
  636.4 23.3 %copy-start.8 = (bf16[128,240]{0,1:T(8,128)(2,1)}, bf16[128,240]{0,1:T(8,128)(2,1)S(1)}, u32[]{:S(2)}) copy-start(bf16[128,240]{0,1:T(8,128)(2,1)S(1)} %add_convert_fusion) | copy-start | bytes 184324
  659.7 1.2 copy-start.2
  678.8 56.0 %all-to-all-start.2 = ((bf16[64,50,256]{2,1,0:T(8,128)(2,1)}), bf16[64,50,256]{2,1,0:T(8,128)(2,1)S(1)}, u32[]{:S(2)}, u32[]{:S(2)}) async-start(bf16[64,50,256]{2,1,0:T(8,128)(2,1)} %convert_element_type.74), calls=%async_computation.3 | async-start | bytes 3670016 | tf_op jit(solution)/shard_map/all_to_all | solution.py:223
  690.2 608.5 %all-reduce.4.cloned.1.call-start = ((), (), s32[]{:S(2)}) async-start(), calls=%async_computation.7 | async-start | bytes 1966080 | tf_op jit(solution)/shard_map/psum | solution.py:237
  758.1 542.8 %copy-start.9 = (f32[128,256]{1,0:T(8,128)}, f32[128,256]{1,0:T(8,128)S(1)}, u32[]{:S(2)}) copy-start(f32[128,256]{1,0:T(8,128)S(1)} %scatter_custom_fusion.3) | copy-start | bytes 393220
Sparse Core Ops, SparseCore 0:
  54.2 268.2 all-gather.6
  324.8 245.4 all-gather.4
  605.4 30.1 reduce-scatter.1
  694.2 604.5 all-reduce.3
where the time goes:
time: 1310 us
  waiting for transfers between devices  1050 us (80%)
  local copies, waits for them, and re-layouts  97.4 us (7%)
  other arithmetic  49.3 us (4%)
  starting transfers between devices  38.1 us (3%)
  matrix products  32.3 us (2%)
  blocking collectives  27.5 us (2%)
  between operations  14.4 us (1%)
    psum x1, waiting for transfers between devices, per_device(): proj_grad = lax.psum(proj_term, 'seq')  541 us
    all_gather x1, waiting for transfers between devices, per_device(): key_piece = lax.all_gather(key_here, 'seq', axis=0, tiled=True)  243 us
    all_gather x1, waiting for transfers between devices, per_device(): value_piece = lax.all_gather(value_here, 'seq', axis=0, tiled=True)  194 us
    all_to_all x1, waiting for transfers between devices, per_device(): lax.all_to_all(outgoing.reshape(seq_count, capacity, target_width).astype...  40.9 us
  transfers between devices with their start and end apart: 9, of which 6 were waited for; matrix products, arithmetic and copies ran while one was open for 10% of the time, Pallas kernels for 0%

commit v1 on v0

--- a/solution.py
+++ b/solution.py
@@ -87,6 +87,17 @@
 def place_rows(asked_flat, rows_flat, frame_count):
     segment_ids = jnp.where(asked_flat >= 0, asked_flat, frame_count)
     return jax.ops.segment_sum(rows_flat, segment_ids, num_segments=frame_count + 1)[:frame_count]
+
+
+def seq_sum(term, axis):
+    size = lax.axis_size(axis)
+    rows, cols = term.shape
+    chunk = -(-rows // size)
+    padded = jnp.pad(term, ((0, chunk * size - rows), (0, 0))).reshape(size, chunk, cols)
+    reduced = lax.all_to_all(padded, axis, 0, 0, tiled=True).sum(axis=0)
+    copies = jnp.broadcast_to(reduced[None], (size, chunk, cols))
+    gathered = lax.all_to_all(copies, axis, 0, 0, tiled=True)
+    return gathered.reshape(size * chunk, cols)[:rows]
 
 
 def per_device(
@@ -135,8 +146,14 @@
         jnp.full((head_count, frame_count), -1e30, jnp.float32),
     )
     running = initial
-    key_piece = lax.all_gather(key_here, "seq", axis=0, tiled=True)
-    value_piece = lax.all_gather(value_here, "seq", axis=0, tiled=True)
+    seq_total = lax.axis_size("seq")
+    kv_here = jnp.concatenate([key_here, value_here], axis=1)
+    kv_copies = jnp.broadcast_to(kv_here[None], (seq_total,) + kv_here.shape).reshape(
+        seq_total * frame_count, 2 * local_width
+    )
+    kv_all = lax.all_to_all(kv_copies, "seq", 0, 0, tiled=True)
+    key_piece = kv_all[:, :local_width]
+    value_piece = kv_all[:, local_width:]
     row_count = key_piece.shape[0]
 
     def advance(partial_value, blocks):
@@ -234,7 +251,7 @@
     proj_term = jnp.einsum(
         "mw,me->we", masked_full.astype(jnp.float32), context_grad, precision=lax.Precision.HIGHEST
     )
-    proj_grad = lax.psum(proj_term, "seq")
+    proj_grad = seq_sum(proj_term, "seq")
     return (encoded, proj_grad, target_grad)
 
 

time: 1310 us -> 536 us (0.41)
  waiting for transfers between devices: 1050 us -> 235 us
  starting transfers between devices: 38.1 us -> 65.5 us
    psum x1 -> x0, waiting for transfers between devices: 541 us -> none  [per_device(): proj_grad = lax.psum(proj_term, 'seq')]
    all_gather x2 -> x0, waiting for transfers between devices: 437 us -> none  [the longest x1 243 us: per_device(): key_piece = lax.all_gather(key_here, 'seq', axis=0, tiled=True)]
    all_to_all x0 -> x3, waiting for transfers between devices: none -> 168 us  [the longest x1 158 us: per_device(): kv_all = lax.all_to_all(kv_copies, 'seq', 0, 0, tiled=True)]
    all_to_all x0 -> x3, starting transfers between devices: none -> 30.2 us  [the longest x1 11.5 us: per_device(): kv_all = lax.all_to_all(kv_copies, 'seq', 0, 0, tiled=True)]
  transfers between devices with their start and end apart: 9 -> 9, of which waited for: 6 -> 6; matrix products, arithmetic and copies ran while one was open for 10% -> 32% of each run, Pallas kernels for 0% -> 0%
where the time goes in v1:
time: 536 us; the launch traced here: 530 us
  waiting for transfers between devices  235 us (44%)
  local copies, waits for them, and re-layouts  105 us (20%)
  starting transfers between devices  65.5 us (12%)
  other arithmetic  48.1 us (9%)
  matrix products  32.4 us (6%)
  blocking collectives  27.9 us (5%)
  between operations  15.2 us (3%)
    all_to_all x1, waiting for transfers between devices, per_device(): kv_all = lax.all_to_all(kv_copies, 'seq', 0, 0, tiled=True)  158 us
    all_to_all x1, waiting for transfers between devices, per_device(): lax.all_to_all(outgoing.reshape(seq_count, capacity, target_width).astype...  43.7 us
    scatter-add x1, other arithmetic, place_rows(): jax.ops.segment_sum(rows_flat, segment_ids, num_segments=frame_count + 1)  20.7 us
    reduce_scatter x1, waiting for transfers between devices, per_device(): lax.psum_scatter(jnp.dot(attended, out_weight, preferred_element_type=jnp...  19.1 us
    another operation x4, other arithmetic  18.4 us
    dynamic_slice x16, local copies, waits for them, and re-layouts, per_device(): lax.scan(advance, running, (key_piece.reshape(row_count // 512, 512, -1),...  17.6 us
    conv_general_dilated x1, matrix products, per_device(): lax.conv_general_dilated(extended[None], conv_weight, (1,), 'VALID', dime...  17.3 us
    psum x1, blocking collectives, per_device(): lax.psum((products_here, target_sq_here, context_sq_here), 'head')  13.5 us
  transfers between devices with their start and end apart: 9, of which 6 were waited for; matrix products, arithmetic and copies ran while one was open for 32% of the time, Pallas kernels for 0%

profile of v1, /device:TPU:8, one launch (start us, length us, event | category | flops | bytes accessed | tf_op | source)
XLA Modules:
  0.0 530.1 jit_solution(13953745539456377871)
XLA Ops:
  16.7 18.1 %reduce-window.6 = s32[64,13,128]{2,1,0:T(8,128)S(1)} reduce-window(s32[64,13,128]{2,1,0:T(8,128)S(1)} %reshape.273, s32[]{:T(128)} %constant.57.clone.1), window={size=1x1x128 pad=0_0x0_0x127_0}, to_apply=%region_7.8 | reduce-window | flops 13524992 | bytes 851972 | tf_op jit(solution)/shard_map/reduce-window
  36.0 8.8 %scatter_custom_fusion = s32[3200]{0:T(1024)S(1)} fusion(s32[1600]{0:T(1024)S(1)} %fusion.54, s32[1600]{0:T(1024)S(1)} %get-tuple-element.120, s32[]{:T(128)} %constant.142.clone.1), kind=kCustom, calls=%fused_computation.115 | custom fusion | bytes 12804 | tf_op jit(solution)/shard_map/scatter | solution.py:208
  45.6 13.1 %all-to-all-start.1 = ((s32[64,1,50]{2,1,0:T(1,128)}), s32[64,1,50]{2,1,0:T(1,128)S(1)}, u32[]{:S(2)}, u32[]{:S(2)}) async-start(s32[64,1,50]{2,1,0:T(1,128)} %bitcast.24), calls=%async_computation.2 | async-start | bytes 65536 | tf_op jit(solution)/shard_map/all_to_all | solution.py:212
  58.7 10.7 %copy.57 = bf16[2,120,120,128]{2,1,0,3:T(8,128)(2,1)} copy(bf16[2,120,120,128]{3,2,1,0:T(8,128)(2,1)} %bitcast.154) | data formatting | bytes 14745600 | tf_op jit(solution)/shard_map/shard_map
  72.8 17.3 %fusion.68 = f32[1,129,2,120]{3,0,2,1:T(1,128)S(1)} fusion(bf16[1,256,2,120]{3,0,2,1:T(2,128)(2,1)S(1)} %copy.56, bf16[2,120,120,128]{2,1,0,3:T(8,128)(2,1)} %copy.57), kind=kOutput, calls=%fused_computation.138 | convolution fusion | flops 951091200 | bytes 7619520 | tf_op jit(solution)/shard_map/conv_general_dilated | solution.py:122
  90.5 7.5 %all_gather.6 = bf16[128,960]{0,1:T(8,128)(2,1)S(1)} all-gather(bf16[128,240]{0,1:T(8,128)(2,1)S(1)} %fusion.22), channel_id=1, replica_groups=mesh['seq'=64,'head'=4] {'head'}, dimensions={1}, use_global_device_ids=true | all-gather | bytes 307200 | tf_op jit(solution)/shard_map/all_gather | solution.py:134
  103.6 11.5 %all-to-all-start = ((bf16[64,128,480]{1,2,0:T(8,128)(2,1)}), bf16[64,128,480]{1,2,0:T(8,128)(2,1)}, u32[]{:S(2)}, u32[]{:S(2)}) async-start(bf16[64,128,480]{1,2,0:T(8,128)(2,1)} %broadcast_in_dim.31), calls=%async_computation | async-start | bytes 15728640 | tf_op jit(solution)/shard_map/all_to_all | solution.py:154
  119.0 9.9 %gather_fusion.2 = bf16[3200,256]{1,0:T(8,128)(2,1)S(1)} fusion(bf16[128,256]{1,0:T(8,128)(2,1)S(1)} %copy-done.1, s32[4096]{0:T(1024)S(1)} %pad_clamp_fusion), kind=kCustom, calls=%fused_computation.2 | custom fusion | bytes 3289600 | tf_op jit(solution)/shard_map/gather | solution.py:84
  131.9 157.9 %all-to-all-done = bf16[64,128,480]{1,2,0:T(8,128)(2,1)} async-done(((bf16[64,128,480]{1,2,0:T(8,128)(2,1)}), bf16[64,128,480]{1,2,0:T(8,128)(2,1)}, u32[]{:S(2)}, u32[]{:S(2)}) %all-to-all-start) | async-done | bytes 7864352 | tf_op jit(solution)/shard_map/all_to_all | solution.py:154
  289.8 8.6 %all-to-all-start.2 = ((bf16[64,50,256]{2,1,0:T(8,128)(2,1)}), bf16[64,50,256]{2,1,0:T(8,128)(2,1)}, u32[]{:S(2)}, u32[]{:S(2)}) async-start(bf16[64,50,256]{2,1,0:T(8,128)(2,1)} %reshape.293), calls=%async_computation.3 | async-start | bytes 3670016 | tf_op jit(solution)/shard_map/all_to_all | solution.py:214
  298.5 4.3 copy_bitcast_fusion
  307.3 29.5 %while.15 = (s32[]{:T(128)}, f32[2,128,120]{1,2,0:T(8,128)S(1)}, f32[2,128]{1,0:T(2,128)S(1)}, f32[2,128]{1,0:T(2,128)S(1)}, bf16[16,512,240]{1,2,0:T(8,128)(2,1...) while((s32[]{:T(128)}, f32[2,128,120]{1,2,0:T(8,128)S(1)}, ...), condition=%wide.region_5.6_spmd.clone, body=%wide.region_2.5_spmd.clone.sunk | while | flops 63794432 | bytes 3371117 | solution.py:165
  338.6 4.7 all-to-all-done.2
  345.8 5.6 %gather_fusion.3 = bf16[1600,256]{1,0:T(8,128)(2,1)S(1)} fusion(bf16[3200,256]{1,0:T(8,128)(2,1)S(1)} %reshape.265, s32[2048]{0:T(1024)S(1)} %pad_clamp_fusion.1), kind=kCustom, calls=%fused_computation.3 | custom fusion | bytes 1644800 | tf_op jit(solution)/shard_map/gather | solution.py:215
  352.0 19.1 %reduce-scatter.2.cloned.1.call-done = bf16[128,240]{0,1:T(8,128)(2,1)} async-done(((bf16[128,960]{0,1:T(8,128)(2,1)}), bf16[128,240]{0,1:T(8,128)(2,1)}) %reduce-scatter.2.cloned.1.call-update) | async-done | bytes 61456 | tf_op jit(solution)/shard_map/reduce_scatter | solution.py:180
  372.7 7.0 %all-gather.1 = bf16[4,240,16]{1,2,0:T(8,128)(2,1)S(1)} all-gather(bf16[1,240,16]{1,2,0:T(8,128)(2,1)S(1)} %bitcast.171), channel_id=2, replica_groups=mesh['seq'=64,'head'=4] {'head'}, dimensions={0}, use_global_device_ids=true | all-gather | bytes 38400 | tf_op jit(solution)/shard_map/all_gather | solution.py:190
  380.8 13.5 %all-reduce.1 = (f32[16,101]{1,0:T(8,128)S(1)}, f32[16]{0:T(128)S(1)}, f32[16,101]{1,0:T(8,128)S(1)}) all-reduce(f32[16,101]{1,0:T(8,128)S(1)} %fusion.7, f32[16]{0:T(128)S(1)} %get-tuple-element.124, f32[16,101]{1,0:T(8,128)S(1)} %bitcast.174), channel_id=1, replica_groups=mesh['seq'=64,'head'=4] {'head'}, use_global_device_ids=true, to_apply=%region_15.16 | all-reduce | flops 3248 | bytes 25984 | tf_op jit(solution)/shard_map/psum | solution.py:222
  397.1 11.5 %all-to-all-start.3 = ((f32[64,15,256]{2,1,0:T(8,128)}), f32[64,15,256]{2,1,0:T(8,128)S(1)}, u32[]{:S(2)}, u32[]{:S(2)}) async-start(f32[64,15,256]{2,1,0:T(8,128)} %reshape.267), calls=%async_computation.4 | async-start | bytes 2097152 | tf_op jit(solution)/shard_map/all_to_all | solution.py:97
  412.0 12.8 %scatter_custom_fusion.1 = f32[3200,256]{1,0:T(8,128)} fusion(s32[1600]{0:T(1024)} %copy-done.10, f32[1600,256]{1,0:T(8,128)} %reshape.320, f32[]{:T(128)} %constant.68.clone.1), kind=kCustom, calls=%fused_computation.30 | custom fusion | bytes 3277312 | tf_op jit(solution)/shard_map/scatter | solution.py:237
  428.3 7.6 %all-to-all-done.3 = f32[64,15,256]{2,1,0:T(8,128)S(1)} async-done(((f32[64,15,256]{2,1,0:T(8,128)}), f32[64,15,256]{2,1,0:T(8,128)S(1)}, u32[]{:S(2)}, u32[]{:S(2)}) %all-to-all-start.3) | async-done | bytes 983072 | tf_op jit(solution)/shard_map/all_to_all | solution.py:97
  435.9 6.8 %all-to-all-start.5 = ((bf16[64,50,256]{2,1,0:T(8,128)(2,1)}), bf16[64,50,256]{2,1,0:T(8,128)(2,1)S(1)}, u32[]{:S(2)}, u32[]{:S(2)}) async-start(bf16[64,50,256]{2,1,0:T(8,128)(2,1)} %convert_element_type.74), calls=%async_computation.6 | async-start | bytes 3670016 | tf_op jit(solution)/shard_map/all_to_all | solution.py:240
  442.8 43.7 %all-to-all-done.5 = bf16[64,50,256]{2,1,0:T(8,128)(2,1)S(1)} async-done(((bf16[64,50,256]{2,1,0:T(8,128)(2,1)}), bf16[64,50,256]{2,1,0:T(8,128)(2,1)S(1)}, u32[]{:S(2)}, u32[]{:S(2)}) %all-to-all-start.5) | async-done | bytes 1638432 | tf_op jit(solution)/shard_map/all_to_all | solution.py:240
  487.7 7.2 %all-to-all-start.4 = ((f32[64,15,256]{2,1,0:T(8,128)}), f32[64,15,256]{2,1,0:T(8,128)S(1)}, u32[]{:S(2)}, u32[]{:S(2)}) async-start(f32[64,15,256]{2,1,0:T(8,128)} %broadcast_in_dim.35), calls=%async_computation.5 | async-start | bytes 2097152 | tf_op jit(solution)/shard_map/all_to_all | solution.py:99
  497.9 20.7 %scatter_custom_fusion.2 = f32[129,256]{1,0:T(8,128)S(1)} fusion(s32[3200]{0:T(1024)S(1)} %fusion.48, f32[3200,256]{1,0:T(8,128)} %reshape.328, f32[]{:T(128)} %constant.68.clone.1), kind=kCustom, calls=%fused_computation.80 | custom fusion | flops 819200 | bytes 132608 | tf_op jit(solution)/shard_map/scatter-add | solution.py:89
  (237 shorter events, 86.3 us)
Async XLA Ops:
  7.2 329.7 %copy-start = (bf16[240,960]{1,0:T(8,128)(2,1)S(1)}, bf16[240,960]{1,0:T(8,128)(2,1)}, u32[]{:S(2)}) copy-start(bf16[240,960]{1,0:T(8,128)(2,1)} %param.22) | copy-start | bytes 1382404
  8.2 64.3 %collective-permute-start = (bf16[64,240]{0,1:T(8,128)(2,1)S(1)}, bf16[64,240]{0,1:T(8,128)(2,1)S(1)}, u32[]{:S(2)}, u32[]{:S(2)}) collective-permute-start(bf16[64,240]{0,1:T(8,128)(2,1)S(1)} %get-tuple-element.115), channel_id=1, source_target_pairs={{0,4},{4,8},{8,12},{12,16},{16,20},{20,24},{24,28},{28,32},{32,36}... | collective-permute-start | bytes 92168 | tf_op jit(solution)/shard_map/ppermute | solution.py:23
  11.6 60.9 %collective-permute-start.1 = (bf16[64,240]{0,1:T(8,128)(2,1)S(1)}, bf16[64,240]{0,1:T(8,128)(2,1)S(1)}, u32[]{:S(2)}, u32[]{:S(2)}) collective-permute-start(bf16[64,240]{0,1:T(8,128)(2,1)S(1)} %get-tuple-element.116), channel_id=1, source_target_pairs={{4,0},{8,4},{12,8},{16,12},{20,16},{24,20},{28,24},{32,28},{36,32}... | collective-permute-start | bytes 92168 | tf_op jit(solution)/shard_map/ppermute | solution.py:24
  36.0 302.6 %copy-start.10 = (s32[1600]{0:T(1024)}, s32[1600]{0:T(1024)S(1)}, u32[]{:S(2)}) copy-start(s32[1600]{0:T(1024)S(1)} %fusion.54) | copy-start | bytes 19204
  45.6 53.8 %all-to-all-start.1 = ((s32[64,1,50]{2,1,0:T(1,128)}), s32[64,1,50]{2,1,0:T(1,128)S(1)}, u32[]{:S(2)}, u32[]{:S(2)}) async-start(s32[64,1,50]{2,1,0:T(1,128)} %bitcast.24), calls=%async_computation.2 | async-start | bytes 65536 | tf_op jit(solution)/shard_map/all_to_all | solution.py:212
  58.6 10.8 %copy-start.5 = (bf16[2,115200]{1,0:T(2,128)(2,1)S(1)}, bf16[2,115200]{1,0:T(2,128)(2,1)}, u32[]{:S(2)}) copy-start(bf16[2,115200]{1,0:T(2,128)(2,1)} %param.20) | copy-start | bytes 1382404
  69.4 1.5 copy-start.6
  69.4 3.1 copy-start.3
  72.8 25.5 %copy-start.12 = (f32[960]{0:T(1024)S(1)}, f32[960]{0:T(1024)}, u32[]{:S(2)}) copy-start(f32[960]{0:T(1024)} %param.18) | copy-start | bytes 11524
  72.8 25.5 %copy-start.13 = (f32[960]{0:T(1024)S(1)}, f32[960]{0:T(1024)}, u32[]{:S(2)}) copy-start(f32[960]{0:T(1024)} %param.17) | copy-start | bytes 11524
  103.6 11.6 %copy-start.7 = (bf16[2,115200]{1,0:T(2,128)(2,1)S(1)}, bf16[2,115200]{1,0:T(2,128)(2,1)}, u32[]{:S(2)}) copy-start(bf16[2,115200]{1,0:T(2,128)(2,1)} %param.19) | copy-start | bytes 1382404
  103.6 186.2 %all-to-all-start = ((bf16[64,128,480]{1,2,0:T(8,128)(2,1)}), bf16[64,128,480]{1,2,0:T(8,128)(2,1)}, u32[]{:S(2)}, u32[]{:S(2)}) async-start(bf16[64,128,480]{1,2,0:T(8,128)(2,1)} %broadcast_in_dim.31), calls=%async_computation | async-start | bytes 15728640 | tf_op jit(solution)/shard_map/all_to_all | solution.py:154
  115.1 3.8 copy-start.1
  289.8 53.5 %all-to-all-start.2 = ((bf16[64,50,256]{2,1,0:T(8,128)(2,1)}), bf16[64,50,256]{2,1,0:T(8,128)(2,1)}, u32[]{:S(2)}, u32[]{:S(2)}) async-start(bf16[64,50,256]{2,1,0:T(8,128)(2,1)} %reshape.293), calls=%async_computation.3 | async-start | bytes 3670016 | tf_op jit(solution)/shard_map/all_to_all | solution.py:214
  298.5 72.6 %reduce-scatter.2.cloned.1.call-start = ((), (), s32[]{:S(2)}) async-start(), calls=%async_computation.7 | async-start | bytes 307200 | tf_op jit(solution)/shard_map/reduce_scatter | solution.py:180
  307.3 30.6 %copy-start.14 = (s32[16]{0:T(128)S(1)}, s32[16]{0:T(128)}, u32[]{:S(2)}) copy-start(s32[16]{0:T(128)} %param.25) | copy-start | bytes 196
  351.4 28.3 %copy-start.4 = (bf16[960,256]{1,0:T(8,128)(2,1)S(1)}, bf16[960,256]{1,0:T(8,128)(2,1)}, u32[]{:S(2)}) copy-start(bf16[960,256]{1,0:T(8,128)(2,1)} %param.23) | copy-start | bytes 1474564
  351.6 43.0 %copy-start.11 = (f32[16]{0:T(128)S(1)}, f32[16]{0:T(128)}, u32[]{:S(2)}) copy-start(f32[16]{0:T(128)} %param.27) | copy-start | bytes 196
  372.0 24.0 %copy-start.8 = (bf16[128,240]{0,1:T(8,128)(2,1)}, bf16[128,240]{0,1:T(8,128)(2,1)S(1)}, u32[]{:S(2)}) copy-start(bf16[128,240]{0,1:T(8,128)(2,1)S(1)} %add_convert_fusion) | copy-start | bytes 184324
  397.1 38.8 %all-to-all-start.3 = ((f32[64,15,256]{2,1,0:T(8,128)}), f32[64,15,256]{2,1,0:T(8,128)S(1)}, u32[]{:S(2)}, u32[]{:S(2)}) async-start(f32[64,15,256]{2,1,0:T(8,128)} %reshape.267), calls=%async_computation.4 | async-start | bytes 2097152 | tf_op jit(solution)/shard_map/all_to_all | solution.py:97
  409.3 1.2 copy-start.2
  435.9 50.7 %all-to-all-start.5 = ((bf16[64,50,256]{2,1,0:T(8,128)(2,1)}), bf16[64,50,256]{2,1,0:T(8,128)(2,1)S(1)}, u32[]{:S(2)}, u32[]{:S(2)}) async-start(bf16[64,50,256]{2,1,0:T(8,128)(2,1)} %convert_element_type.74), calls=%async_computation.6 | async-start | bytes 3670016 | tf_op jit(solution)/shard_map/all_to_all | solution.py:240
  487.7 34.0 %all-to-all-start.4 = ((f32[64,15,256]{2,1,0:T(8,128)}), f32[64,15,256]{2,1,0:T(8,128)S(1)}, u32[]{:S(2)}, u32[]{:S(2)}) async-start(f32[64,15,256]{2,1,0:T(8,128)} %broadcast_in_dim.35), calls=%async_computation.5 | async-start | bytes 2097152 | tf_op jit(solution)/shard_map/all_to_all | solution.py:99
  519.4 3.3 copy-start.9
Sparse Core Ops, SparseCore 0:
  338.0 33.0 reduce-scatter.1
